TPU v7x, 128 devices: a whole 4x4x4 slice. The times are simulated.
128 devices in a mesh: ctx: 32 (over z, y_hi, x), ch: 4 (over y_lo, core).
Axes of the slice: x: 4, y: 4 (y_hi: 2, y_lo: 2; y = y_hi * 2 + y_lo), z: 4, core: 2. Of those that a mesh axis runs over, the one named last changes fastest.
Arguments:
- q_conv: bfloat16 [7168, 4096], P('ctx', 'ch'), may hold values from -6 to 6
- k_conv: bfloat16 [7168, 4096], P('ctx', 'ch'), may hold values from -6 to 6
- v_conv: bfloat16 [7168, 4096], P('ctx', 'ch'), may hold values from -6 to 6
- conv_filter: bfloat16 [7168, 256], P('ctx', 'ch'), may hold values from -1 to 1
- q_attn: bfloat16 [7168, 4096], P('ctx', 'ch'), may hold values from -5 to 5
- k_attn: bfloat16 [7168, 4096], P('ctx', 'ch'), may hold values from -5 to 5
- v_attn: bfloat16 [7168, 4096], P('ctx', 'ch'), may hold values from -6 to 6
- w_conv_out: bfloat16 [4096, 4096], P('ch'), may hold values from -0.09375 to 0.09375
- w_attn_out: bfloat16 [4096, 4096], P('ch'), may hold values from -0.375 to 0.375
Outputs:
- layer_out: bfloat16 [7168, 4096], P(('ctx', 'ch'))
All inputs are finite; a program needn't handle non-finite values.
Results may differ from a plain program's by a relative error of at most 0.018.
Values may be sent and summed in bfloat16 or wider, within the bound.
No kernel may reach another device: no remote copies, remote signals or barrier semaphores. Data moves between devices by JAX's collectives and lax.ppermute only.
A program may use at most 192 MiB of HBM per device.

v0:
```python
from functools import partial
import math
import jax
import jax.numpy as jnp
from jax import lax
from jax.sharding import PartitionSpec as P

HD = 128
two_pi = 2.0 * math.pi
neg_large = -1e30
highest = lax.Precision.HIGHEST


def angle_table(left_idx, right_idx, period):
    product = left_idx[:, None] * right_idx[None, :] % period
    return product.astype(jnp.float32) * (two_pi / period)


def section_coarse(values, cos_table, sin_table, twiddle):
    real_part = jnp.einsum("kn,nsc->ksc", cos_table, values, precision=highest)
    imag_part = -jnp.einsum("kn,nsc->ksc", sin_table, values, precision=highest)
    cos_twist = jnp.cos(twiddle)[:, :, None]
    sin_twist = jnp.sin(twiddle)[:, :, None]
    return (
        real_part * cos_twist + imag_part * sin_twist,
        imag_part * cos_twist - real_part * sin_twist,
    )


def section_fine(real_part, imag_part, cos_table, sin_table, direction):
    cos_real = jnp.einsum("kn,anc->akc", cos_table, real_part, precision=highest)
    cos_imag = jnp.einsum("kn,anc->akc", cos_table, imag_part, precision=highest)
    sin_real = jnp.einsum("kn,anc->akc", sin_table, real_part, precision=highest)
    sin_imag = jnp.einsum("kn,anc->akc", sin_table, imag_part, precision=highest)
    return (cos_real - direction * sin_imag, cos_imag + direction * sin_real)


def spectral_conv(gated, filters, my_index, tok_rows, count_ctx):
    chans = gated.shape[1]
    groups = filters.shape[1]
    share = chans // groups
    sub_rows = tok_rows // count_ctx
    period = 2 * count_ctx * tok_rows
    got_source, got_filter = (
        lax.all_to_all(
            gated.reshape(1, tok_rows, chans), "ctx", split_axis=1, concat_axis=0, tiled=True
        ),
        lax.all_to_all(
            filters.reshape(1, tok_rows, groups), "ctx", split_axis=1, concat_axis=0, tiled=True
        ),
    )
    coarse_idx = jnp.arange(count_ctx, dtype=jnp.int32)
    coarse_freq = jnp.arange(2 * count_ctx, dtype=jnp.int32)
    coarse_angle = angle_table(coarse_freq, coarse_idx, 2 * count_ctx)
    cos_coarse = jnp.cos(coarse_angle)
    sin_coarse = jnp.sin(coarse_angle)
    fine_global = my_index * sub_rows + jnp.arange(sub_rows, dtype=jnp.int32)
    twist_in = angle_table(coarse_freq, fine_global, period)
    source_re, source_im = section_coarse(
        got_source.astype(jnp.float32), cos_coarse, sin_coarse, twist_in
    )
    filter_re, filter_im = section_coarse(
        got_filter.astype(jnp.float32), cos_coarse, sin_coarse, twist_in
    )
    source_re, source_im, filter_re, filter_im = (
        lax.all_to_all(
            source_re.astype(jnp.bfloat16), "ctx", split_axis=0, concat_axis=1, tiled=True
        ).astype(source_re.dtype),
        lax.all_to_all(
            source_im.astype(jnp.bfloat16), "ctx", split_axis=0, concat_axis=1, tiled=True
        ).astype(source_im.dtype),
        lax.all_to_all(
            filter_re.astype(jnp.bfloat16), "ctx", split_axis=0, concat_axis=1, tiled=True
        ).astype(filter_re.dtype),
        lax.all_to_all(
            filter_im.astype(jnp.bfloat16), "ctx", split_axis=0, concat_axis=1, tiled=True
        ).astype(filter_im.dtype),
    )
    fine_idx = jnp.arange(tok_rows, dtype=jnp.int32)
    fine_angle = angle_table(fine_idx, fine_idx, tok_rows)
    cos_fine = jnp.cos(fine_angle)
    sin_fine = jnp.sin(fine_angle)
    source_re, source_im = section_fine(source_re, source_im, cos_fine, sin_fine, -1.0)
    filter_re, filter_im = section_fine(filter_re, filter_im, cos_fine, sin_fine, -1.0)
    split_re = source_re.reshape(2, tok_rows, groups, share)
    split_im = source_im.reshape(2, tok_rows, groups, share)
    prod_re = split_re * filter_re[..., None] - split_im * filter_im[..., None]
    prod_im = split_re * filter_im[..., None] + split_im * filter_re[..., None]
    back_re, back_im = section_fine(
        prod_re.reshape(2, tok_rows, chans),
        prod_im.reshape(2, tok_rows, chans),
        cos_fine,
        sin_fine,
        1.0,
    )
    pair_freq = my_index * 2 + jnp.arange(2, dtype=jnp.int32)
    twist_out = angle_table(pair_freq, fine_idx, period)
    cos_out = jnp.cos(twist_out)[:, :, None]
    sin_out = jnp.sin(twist_out)[:, :, None]
    turned_re = back_re * cos_out - back_im * sin_out
    turned_im = back_re * sin_out + back_im * cos_out
    turned_re, turned_im = (
        lax.all_to_all(
            turned_re.astype(jnp.bfloat16), "ctx", split_axis=1, concat_axis=0, tiled=True
        ).astype(turned_re.dtype),
        lax.all_to_all(
            turned_im.astype(jnp.bfloat16), "ctx", split_axis=1, concat_axis=0, tiled=True
        ).astype(turned_im.dtype),
    )
    result = jnp.einsum("nk,ksc->nsc", cos_coarse.T, turned_re, precision=highest)
    result = result - jnp.einsum("nk,ksc->nsc", sin_coarse.T, turned_im, precision=highest)
    rounded = (result / period).astype(jnp.bfloat16)
    returned = lax.all_to_all(rounded, "ctx", split_axis=0, concat_axis=1, tiled=True)
    return returned.reshape(tok_rows, chans)


def keep_same(running):
    return running


def attend_block(group_query, group_pos, key_block, value_block, key_pos, score_scale, group_state):
    run_max, run_total, run_accum = group_state
    scores = (
        jnp.einsum("thd,shd->hts", group_query, key_block, preferred_element_type=jnp.float32)
        * score_scale
    )
    allowed = (key_pos[None, :] <= group_pos[:, None])[None]
    block_max = jnp.max(jnp.where(allowed, scores, neg_large), axis=2)
    new_max = jnp.maximum(run_max, block_max)
    factor = jnp.exp(run_max - new_max)
    weights = jnp.where(allowed, jnp.exp(scores - new_max[:, :, None]), 0.0)
    new_total = run_total * factor + jnp.sum(weights, axis=2)
    new_accum = run_accum * factor[:, :, None] + jnp.einsum(
        "hts,shd->htd",
        weights.astype(jnp.bfloat16),
        value_block,
        preferred_element_type=jnp.float32,
    )
    return (new_max, new_total, new_accum)


def attention(q_attn, k_attn, v_attn, my_index, tok_rows):
    heads_local = q_attn.shape[1] // HD
    score_scale = HD ** (-0.5)
    queries = q_attn.reshape(tok_rows, heads_local, HD)
    group_list = [(queries, my_index * tok_rows + jnp.arange(tok_rows, dtype=jnp.int32))]
    initial = tuple(
        (
            (
                jnp.full((heads_local, entry[0].shape[0]), neg_large, jnp.float32),
                jnp.zeros((heads_local, entry[0].shape[0]), jnp.float32),
                jnp.zeros((heads_local, entry[0].shape[0], HD), jnp.float32),
            )
            for entry in group_list
        )
    )
    key_piece = lax.all_gather(k_attn, "ctx", axis=0, tiled=True)
    value_piece = lax.all_gather(v_attn, "ctx", axis=0, tiled=True)
    count_blocks = key_piece.shape[0] // tok_rows
    keys_split = key_piece.reshape(count_blocks, tok_rows, heads_local, HD)
    values_split = value_piece.reshape(count_blocks, tok_rows, heads_local, HD)

    def one_block(carry, item):
        key_block, value_block, block_number = item
        block_first = block_number * tok_rows
        key_pos = block_first + jnp.arange(tok_rows, dtype=jnp.int32)
        updated = []
        for entry, group_state in zip(group_list, carry):
            step_fn = partial(
                attend_block, entry[0], entry[1], key_block, value_block, key_pos, score_scale
            )
            updated.append(lax.cond(block_first <= entry[1][-1], step_fn, keep_same, group_state))
        return (tuple(updated), None)

    new_state, unused = lax.scan(
        one_block, initial, (keys_split, values_split, jnp.arange(count_blocks, dtype=jnp.int32))
    )
    outputs = [
        (state[2] / state[1][:, :, None]).transpose(1, 0, 2).astype(jnp.bfloat16)
        for state in new_state
    ]
    merged = outputs[0]
    return merged.reshape(tok_rows, heads_local * HD)


def local(q_conv, k_conv, v_conv, conv_filter, q_attn, k_attn, v_attn, w_conv_out, w_attn_out):
    count_ctx = lax.axis_size("ctx")
    my_index = lax.axis_index("ctx")
    tok_rows = q_conv.shape[0]
    gated = (k_conv.astype(jnp.float32) * v_conv.astype(jnp.float32)).astype(jnp.bfloat16)
    conv = spectral_conv(gated, conv_filter, my_index, tok_rows, count_ctx)
    mixed = (q_conv.astype(jnp.float32) * conv.astype(jnp.float32)).astype(jnp.bfloat16)
    attended = attention(q_attn, k_attn, v_attn, my_index, tok_rows)
    return lax.psum_scatter(
        (
            jnp.dot(mixed, w_conv_out, preferred_element_type=jnp.float32)
            + jnp.dot(attended, w_attn_out, preferred_element_type=jnp.float32)
        ).astype(jnp.bfloat16),
        "ch",
        scatter_dimension=0,
        tiled=True,
    )


def solution(mesh):
    return jax.shard_map(
        local,
        mesh=mesh,
        in_specs=(
            P("ctx", "ch"),
            P("ctx", "ch"),
            P("ctx", "ch"),
            P("ctx", "ch"),
            P("ctx", "ch"),
            P("ctx", "ch"),
            P("ctx", "ch"),
            P("ch", None),
            P("ch", None),
        ),
        out_specs=P(("ctx", "ch"), None),
        check_vma=False,
    )
```

profile of v0, /device:TPU:1, one launch (start us, length us, event | category | flops | bytes accessed | tf_op | source)
XLA Modules:
  0.0 611.6 jit_solution(7817200553837334792)
XLA Ops:
  11.1 11.3 %all-to-all-start.3 = ((bf16[32,2,224]{2,1,0:T(2,128)(2,1)}), bf16[32,2,224]{2,1,0:T(2,128)(2,1)S(1)}, u32[]{:S(2)}, u32[]{:S(2)}) async-start(bf16[32,2,224]{2,1,0:T(2,128)(2,1)} %reshape.188), calls=%async_computation.3 | async-start | bytes 65536 | tf_op jit(solution)/shard_map/all_to_all | solution.py:48
  24.6 3.3 reduce.5
  31.3 7.0 %all-to-all-start = ((bf16[32,2,3584]{2,1,0:T(2,128)(2,1)}), bf16[32,2,3584]{2,1,0:T(2,128)(2,1)S(1)}, u32[]{:S(2)}, u32[]{:S(2)}) async-start(bf16[32,2,3584]{2,1,0:T(2,128)(2,1)} %reshape.194), calls=%async_computation | async-start | bytes 917504 | tf_op jit(solution)/shard_map/all_to_all | solution.py:45
  41.2 7.5 %all-to-all-done = bf16[32,2,3584]{2,1,0:T(2,128)(2,1)S(1)} async-done(((bf16[32,2,3584]{2,1,0:T(2,128)(2,1)}), bf16[32,2,3584]{2,1,0:T(2,128)(2,1)S(1)}, u32[]{:S(2)}, u32[]{:S(2)}) %all-to-all-start) | async-done | bytes 458784 | tf_op jit(solution)/shard_map/all_to_all | solution.py:45
  48.7 4.4 all-to-all-start.5
  57.7 5.0 all-to-all-done.5
  62.7 4.3 all-to-all-start.4
  71.2 5.3 all-to-all-done.4
  76.5 4.1 all-to-all-start.1
  83.0 19.3 %all-to-all-done.1 = bf16[64,7,1024]{2,1,0:T(8,128)(2,1)S(1)} async-done(((bf16[64,7,1024]{2,1,0:T(8,128)(2,1)}), bf16[64,7,1024]{2,1,0:T(8,128)(2,1)S(1)}, u32[]{:S(2)}, u32[]{:S(2)}) %all-to-all-start.1) | async-done | bytes 917536 | tf_op jit(solution)/shard_map/all_to_all | solution.py:66
  102.2 5.0 all-to-all-start.2
  118.6 6.3 %all-to-all-done.2 = bf16[64,7,1024]{2,1,0:T(8,128)(2,1)} async-done(((bf16[64,7,1024]{2,1,0:T(8,128)(2,1)}), bf16[64,7,1024]{2,1,0:T(8,128)(2,1)}, u32[]{:S(2)}, u32[]{:S(2)}) %all-to-all-start.2) | async-done | bytes 917536 | tf_op jit(solution)/shard_map/all_to_all | solution.py:69
  135.4 2.9 fusion.55
  138.2 2.7 fusion.53
  140.9 2.7 convolution_add_fusion.2
  143.6 3.8 fusion.29
  149.3 4.2 all-to-all-start.7
  155.4 10.4 %all-to-all-done.7 = bf16[2,224,1024]{2,0,1:T(2,128)(2,1)S(1)} async-done(((bf16[2,224,1024]{2,0,1:T(2,128)(2,1)}), bf16[2,224,1024]{2,0,1:T(2,128)(2,1)S(1)}, u32[]{:S(2)}, u32[]{:S(2)}) %all-to-all-start.7) | async-done | bytes 917536 | tf_op jit(solution)/shard_map/all_to_all | solution.py:106
  165.8 6.0 all-to-all-start.6
  172.7 19.2 %all-to-all-done.6 = bf16[2,224,1024]{2,0,1:T(2,128)(2,1)S(1)} async-done(((bf16[2,224,1024]{2,0,1:T(2,128)(2,1)}), bf16[2,224,1024]{2,0,1:T(2,128)(2,1)S(1)}, u32[]{:S(2)}, u32[]{:S(2)}) %all-to-all-start.6) | async-done | bytes 917536 | tf_op jit(solution)/shard_map/all_to_all | solution.py:103
  195.3 5.5 all-to-all-start.8
  201.0 10.9 %all-to-all-done.8 = bf16[32,7,1024]{2,1,0:T(8,128)(2,1)S(1)} async-done(((bf16[32,7,1024]{2,1,0:T(8,128)(2,1)}), bf16[32,7,1024]{2,1,0:T(8,128)(2,1)S(1)}, u32[]{:S(2)}, u32[]{:S(2)}) %all-to-all-start.8) | async-done | bytes 458784 | tf_op jit(solution)/shard_map/all_to_all | solution.py:113
  212.0 7.3 %fusion.37 = f32[224,4096]{1,0:T(8,128)} fusion(bf16[1024,4096]{1,0:T(8,128)(2,1)} %param.20, f32[224,1024]{1,0:T(8,128)S(1)} %reshape.181, bf16[224,1024]{1,0:T(8,128)(2,1)S(1)} %copy-done.6), kind=kOutput, calls=%fused_computation.63 | convolution fusion | flops 1879736320 | bytes 13434880 | tf_op jit(solution)/shard_map/dot_general | solution.py:196
  219.3 9.2 %copy.126 = bf16[896,8,8,128]{3,2,1,0:T(8,128)(2,1)S(1)} copy(bf16[896,8,8,128]{3,1,2,0:T(8,128)(2,1)} %bitcast.171) | data formatting | bytes 29360128
  228.6 7.3 %copy.117 = bf16[32,224,8,128]{3,1,2,0:T(8,128)(2,1)} copy(bf16[32,224,8,128]{3,2,1,0:T(8,128)(2,1)S(1)} %bitcast.169) | data formatting | bytes 29360128 | tf_op jit(solution)/shard_map/while | solution.py:175
  235.9 97.1 %all-gather.5.cloned.1.call-done = bf16[7168,1024]{1,0:T(8,128)(2,1)} async-done(((bf16[224,1024]{1,0:T(8,128)(2,1)}), bf16[7168,1024]{1,0:T(8,128)(2,1)}) %all-gather.5.cloned.1.call-update) | async-done | bytes 14680080 | tf_op jit(solution)/shard_map/all_gather | solution.py:158
  333.0 9.1 %copy.127 = bf16[896,8,8,128]{3,2,1,0:T(8,128)(2,1)S(1)} copy(bf16[896,8,8,128]{3,1,2,0:T(8,128)(2,1)} %bitcast.172) | data formatting | bytes 29360128
  342.1 7.3 %copy.119 = bf16[32,224,8,128]{3,1,2,0:T(8,128)(2,1)} copy(bf16[32,224,8,128]{3,2,1,0:T(8,128)(2,1)S(1)} %bitcast.170) | data formatting | bytes 29360128 | tf_op jit(solution)/shard_map/while | solution.py:175
  349.5 92.0 %while.14 = (s32[]{:T(128)}, f32[8,224]{1,0:T(8,128)S(1)}, f32[8,224]{1,0:T(8,128)S(1)}, f32[8,224,128]{2,1,0:T(8,128)S(1)}, s32[32]{0:T(128)S(1)}, /*index=5*/s...) while((s32[]{:T(128)}, f32[8,224]{1,0:T(8,128)S(1)}, ...), condition=%wide.region_5.6_spmd, body=%wide.region_0.5_spmd.sunk | while | flops 210449120 | bytes 8349359 | solution.py:175
  352.2 4.2 conditional.2
  441.5 7.9 %fusion.19 = bf16[224,4096]{1,0:T(8,128)(2,1)} fusion(f32[224,4096]{1,0:T(8,128)} %fusion.37, bf16[1024,4096]{1,0:T(8,128)(2,1)} %param.21, f32[8,224,128]{2,1,0:T(8,128)S(1)} %get-tuple-element.145, f32[8,224]{1,0:T(8,128)S(1)} %get-tuple-element.146), kind=kOutput, calls=%fused_computation.26 | convolution fusion | flops 1881341952 | bytes 14818304 | tf_op jit(solution)/shard_map/dot_general | solution.py:197
  449.4 155.4 %reduce-scatter.2.cloned.1.call-done = bf16[56,4096]{1,0:T(8,128)(2,1)} async-done(((bf16[224,4096]{1,0:T(8,128)(2,1)}), bf16[56,4096]{1,0:T(8,128)(2,1)}) %reduce-scatter.2.cloned.1.call-update) | async-done | bytes 458768 | tf_op jit(solution)/shard_map/reduce_scatter | solution.py:194
  (220 shorter events, 100.9 us)
Async XLA Ops:
  6.5 194.3 %copy-start = (bf16[224,1024]{1,0:T(8,128)(2,1)S(1)}, bf16[224,1024]{1,0:T(8,128)(2,1)}, u32[]{:S(2)}) copy-start(bf16[224,1024]{1,0:T(8,128)(2,1)} %param.17) | copy-start | bytes 1376260
  6.5 212.8 %all-gather.3.cloned.1.call-start = ((), (), s32[]{:S(2)}) async-start(), calls=%async_computation.10 | async-start | bytes 15138816 | tf_op jit(solution)/shard_map/all_gather | solution.py:157
  7.3 325.7 %all-gather.5.cloned.1.call-start = ((), (), s32[]{:S(2)}) async-start(), calls=%async_computation.11 | async-start | bytes 15138816 | tf_op jit(solution)/shard_map/all_gather | solution.py:158
  11.1 20.2 %all-to-all-start.3 = ((bf16[32,2,224]{2,1,0:T(2,128)(2,1)}), bf16[32,2,224]{2,1,0:T(2,128)(2,1)S(1)}, u32[]{:S(2)}, u32[]{:S(2)}) async-start(bf16[32,2,224]{2,1,0:T(2,128)(2,1)} %reshape.188), calls=%async_computation.3 | async-start | bytes 65536 | tf_op jit(solution)/shard_map/all_to_all | solution.py:48
  31.3 17.5 %all-to-all-start = ((bf16[32,2,3584]{2,1,0:T(2,128)(2,1)}), bf16[32,2,3584]{2,1,0:T(2,128)(2,1)S(1)}, u32[]{:S(2)}, u32[]{:S(2)}) async-start(bf16[32,2,3584]{2,1,0:T(2,128)(2,1)} %reshape.194), calls=%async_computation | async-start | bytes 917504 | tf_op jit(solution)/shard_map/all_to_all | solution.py:45
  48.7 14.0 %all-to-all-start.5 = ((bf16[32,2,448]{2,1,0:T(2,128)(2,1)}), bf16[32,2,448]{2,1,0:T(2,128)(2,1)S(1)}, u32[]{:S(2)}, u32[]{:S(2)}) async-start(bf16[32,2,448]{2,1,0:T(2,128)(2,1)} %reshape.192), calls=%async_computation.5 | async-start | bytes 131072 | tf_op jit(solution)/shard_map/all_to_all | solution.py:75
  62.7 13.8 %all-to-all-start.4 = ((bf16[32,2,448]{2,1,0:T(2,128)(2,1)}), bf16[32,2,448]{2,1,0:T(2,128)(2,1)S(1)}, u32[]{:S(2)}, u32[]{:S(2)}) async-start(bf16[32,2,448]{2,1,0:T(2,128)(2,1)} %reshape.190), calls=%async_computation.4 | async-start | bytes 131072 | tf_op jit(solution)/shard_map/all_to_all | solution.py:72
  71.2 10.2 %copy-start.5 = (bf16[64,7,1024]{2,0,1:T(8,128)(2,1)S(1)}, bf16[64,7,1024]{2,0,1:T(8,128)(2,1)}, u32[]{:S(2)}) copy-start(bf16[64,7,1024]{2,0,1:T(8,128)(2,1)} %get-tuple-element.199) | copy-start | bytes 2752516
  76.5 25.7 %all-to-all-start.1 = ((bf16[64,7,1024]{2,1,0:T(8,128)(2,1)}), bf16[64,7,1024]{2,1,0:T(8,128)(2,1)S(1)}, u32[]{:S(2)}, u32[]{:S(2)}) async-start(bf16[64,7,1024]{2,1,0:T(8,128)(2,1)} %copy.89), calls=%async_computation.1 | async-start | bytes 2097152 | tf_op jit(solution)/shard_map/all_to_all | solution.py:66
  102.2 6.2 %copy-start.4 = (bf16[64,7,1024]{2,1,0:T(8,128)(2,1)}, bf16[64,7,1024]{2,1,0:T(8,128)(2,1)S(1)}, u32[]{:S(2)}) copy-start(bf16[64,7,1024]{2,1,0:T(8,128)(2,1)S(1)} %all-to-all-done.1) | copy-start | bytes 2752516
  102.2 22.6 %all-to-all-start.2 = ((bf16[64,7,1024]{2,1,0:T(8,128)(2,1)}), bf16[64,7,1024]{2,1,0:T(8,128)(2,1)}, u32[]{:S(2)}, u32[]{:S(2)}) async-start(bf16[64,7,1024]{2,1,0:T(8,128)(2,1)} %copy.92), calls=%async_computation.2 | async-start | bytes 2097152 | tf_op jit(solution)/shard_map/all_to_all | solution.py:69
  130.8 2.0 copy-start.2
  130.8 2.0 copy-start.3
  149.3 16.5 %all-to-all-start.7 = ((bf16[2,224,1024]{2,0,1:T(2,128)(2,1)}), bf16[2,224,1024]{2,0,1:T(2,128)(2,1)S(1)}, u32[]{:S(2)}, u32[]{:S(2)}) async-start(bf16[2,224,1024]{2,0,1:T(2,128)(2,1)} %copy.114), calls=%async_computation.7 | async-start | bytes 1835008 | tf_op jit(solution)/shard_map/all_to_all | solution.py:106
  165.8 26.2 %all-to-all-start.6 = ((bf16[2,224,1024]{2,0,1:T(2,128)(2,1)}), bf16[2,224,1024]{2,0,1:T(2,128)(2,1)S(1)}, u32[]{:S(2)}, u32[]{:S(2)}) async-start(bf16[2,224,1024]{2,0,1:T(2,128)(2,1)} %copy.112), calls=%async_computation.6 | async-start | bytes 1835008 | tf_op jit(solution)/shard_map/all_to_all | solution.py:103
  195.3 16.7 %copy-start.6 = (bf16[224,1024]{1,0:T(8,128)(2,1)S(1)}, bf16[224,1024]{1,0:T(8,128)(2,1)}, u32[]{:S(2)}) copy-start(bf16[224,1024]{1,0:T(8,128)(2,1)} %param.13) | copy-start | bytes 1376260
  195.3 16.6 %all-to-all-start.8 = ((bf16[32,7,1024]{2,1,0:T(8,128)(2,1)}), bf16[32,7,1024]{2,1,0:T(8,128)(2,1)S(1)}, u32[]{:S(2)}, u32[]{:S(2)}) async-start(bf16[32,7,1024]{2,1,0:T(8,128)(2,1)} %copy.116), calls=%async_computation.8 | async-start | bytes 1048576 | tf_op jit(solution)/shard_map/all_to_all | solution.py:113
  200.8 404.0 %reduce-scatter.2.cloned.1.call-start = ((), (), s32[]{:S(2)}) async-start(), calls=%async_computation.12 | async-start | bytes 2293760 | tf_op jit(solution)/shard_map/reduce_scatter | solution.py:194
  441.5 163.3 %copy-start.1 = (bf16[224,1024]{1,0:T(8,128)(2,1)S(1)}, bf16[224,1024]{1,0:T(8,128)(2,1)}, u32[]{:S(2)}) copy-start(bf16[224,1024]{1,0:T(8,128)(2,1)} %param.17) | copy-start | bytes 1376260
Sparse Core Ops, SparseCore 0:
  10.4 179.5 all-gather.2
  193.1 139.8 all-gather.4
  449.5 155.2 reduce-scatter.1
where the time goes:
time: 622 us; the launch traced here: 612 us
  waiting for transfers between devices  340 us (55%)
  local copies, waits for them, and re-layouts  104 us (17%)
  starting transfers between devices  51.9 us (8%)
  matrix products  49.7 us (8%)
  loops' own time  45.7 us (7%)
  between operations  13.9 us (2%)
  other arithmetic  6.44 us (1%)
    reduce_scatter x1, waiting for transfers between devices, local(): lax.psum_scatter((jnp.dot(mixed, w_conv_out, preferred_element_type=jnp.f...  155 us
    all_gather x1, waiting for transfers between devices, attention(): value_piece = lax.all_gather(v_attn, 'ctx', axis=0, tiled=True)  97.1 us
    another operation x1, loops' own time, attention(): lax.scan(one_block, initial, (keys_split, values_split, jnp.arange(count_...  45.1 us
    unnamed x25, local copies, waits for them, and re-layouts  23 us
    dynamic_slice x32, local copies, waits for them, and re-layouts, attention(): lax.scan(one_block, initial, (keys_split, values_split, jnp.arange(count_...  21.2 us
    slice x32, local copies, waits for them, and re-layouts, one_block(): entry[1][-1]  20.8 us
    all_to_all x1, waiting for transfers between devices, spectral_conv(): lax.all_to_all(source_re.astype(jnp.bfloat16), 'ctx', split_axis=0, conca...  19.3 us
    all_to_all x1, waiting for transfers between devices, spectral_conv(): lax.all_to_all(turned_re.astype(jnp.bfloat16), 'ctx', split_axis=1, conca...  19.2 us
  transfers between devices with their start and end apart: 12, of which 11 were waited for; matrix products, arithmetic and copies ran while one was open for 14% of the time, Pallas kernels for 0%

commit v1 on v0

--- a/solution.py
+++ b/solution.py
@@ -155,7 +155,10 @@
         )
     )
     key_piece = lax.all_gather(k_attn, "ctx", axis=0, tiled=True)
-    value_piece = lax.all_gather(v_attn, "ctx", axis=0, tiled=True)
+    size = lax.axis_size("ctx")
+    blocks = jnp.stack([v_attn for _ in range(size)])
+    blocks = lax.all_to_all(blocks, "ctx", split_axis=0, concat_axis=0)
+    value_piece = jnp.concatenate(blocks, axis=0)
     count_blocks = key_piece.shape[0] // tok_rows
     keys_split = key_piece.reshape(count_blocks, tok_rows, heads_local, HD)
     values_split = value_piece.reshape(count_blocks, tok_rows, heads_local, HD)

time: 622 us -> 738 us (1.19)
  waiting for transfers between devices: 340 us -> 438 us
  blocking collectives: 0 us -> 16.6 us
    all_to_all x1, waiting for transfers between devices: 10.9 us -> 189 us  [attention(): blocks = lax.all_to_all(blocks, 'ctx', split_axis=0, concat_axis=0)]
    all_gather x1 -> x0, waiting for transfers between devices: 97.1 us -> none  [attention(): value_piece = lax.all_gather(v_attn, 'ctx', axis=0, tiled=True)]
    reduce_scatter x1, waiting for transfers between devices: 155 us -> 175 us  [local(): lax.psum_scatter((jnp.dot(mixed, w_conv_out, preferred_element_type=jnp.f...]
    all_to_all x0 -> x1, blocking collectives: none -> 16.6 us  [spectral_conv(): lax.all_to_all(rounded, 'ctx', split_axis=0, concat_axis=1, tiled=True)]
    all_to_all x1, waiting for transfers between devices: 19.2 us -> 10.4 us  [spectral_conv(): lax.all_to_all(turned_re.astype(jnp.bfloat16), 'ctx', split_axis=1, conca...]
    unnamed x25 -> x26, local copies, waits for them, and re-layouts: 23 us -> 14.5 us
    all_to_all x1, waiting for transfers between devices: 10.4 us -> 17.8 us  [spectral_conv(): lax.all_to_all(turned_im.astype(jnp.bfloat16), 'ctx', split_axis=1, conca...]
  transfers between devices with their start and end apart: 12 -> 11, of which waited for: 11 -> 10; matrix products, arithmetic and copies ran while one was open for 14% -> 13% of each run, Pallas kernels for 0% -> 0%
where the time goes in v1:
time: 738 us; the launch traced here: 727 us
  waiting for transfers between devices  438 us (59%)
  local copies, waits for them, and re-layouts  107 us (14%)
  starting transfers between devices  51.6 us (7%)
  matrix products  49.8 us (7%)
  loops' own time  43 us (6%)
  blocking collectives  16.6 us (2%)
  between operations  14.2 us (2%)
    all_to_all x1, waiting for transfers between devices, attention(): blocks = lax.all_to_all(blocks, 'ctx', split_axis=0, concat_axis=0)  189 us
    reduce_scatter x1, waiting for transfers between devices, local(): lax.psum_scatter((jnp.dot(mixed, w_conv_out, preferred_element_type=jnp.f...  175 us
    another operation x1, loops' own time, attention(): lax.scan(one_block, initial, (keys_split, values_split, jnp.arange(count_...  42.6 us
    while x3, local copies, waits for them, and re-layouts, attention(): lax.scan(one_block, initial, (keys_split, values_split, jnp.arange(count_...  21.8 us
    dynamic_slice x32, local copies, waits for them, and re-layouts, attention(): lax.scan(one_block, initial, (keys_split, values_split, jnp.arange(count_...  21 us
    slice x32, local copies, waits for them, and re-layouts, one_block(): entry[1][-1]  19.6 us
    all_to_all x1, waiting for transfers between devices, spectral_conv(): lax.all_to_all(turned_im.astype(jnp.bfloat16), 'ctx', split_axis=1, conca...  17.8 us
    all_to_all x1, waiting for transfers between devices, spectral_conv(): lax.all_to_all(source_re.astype(jnp.bfloat16), 'ctx', split_axis=0, conca...  17.3 us
  transfers between devices with their start and end apart: 11, of which 10 were waited for; matrix products, arithmetic and copies ran while one was open for 13% of the time, Pallas kernels for 0%

profile of v1, /device:TPU:1, one launch (start us, length us, event | category | flops | bytes accessed | tf_op | source)
XLA Modules:
  0.0 727.3 jit_solution(17675321367677039023)
XLA Ops:
  10.3 11.3 %all-to-all-start.3 = ((bf16[32,2,224]{2,1,0:T(2,128)(2,1)}), bf16[32,2,224]{2,1,0:T(2,128)(2,1)S(1)}, u32[]{:S(2)}, u32[]{:S(2)}) async-start(bf16[32,2,224]{2,1,0:T(2,128)(2,1)} %reshape.186), calls=%async_computation.3 | async-start | bytes 65536 | tf_op jit(solution)/shard_map/all_to_all | solution.py:48
  23.9 3.3 reduce.5
  30.4 7.1 all-to-all-start
  40.5 7.5 %all-to-all-done = bf16[32,2,3584]{2,1,0:T(2,128)(2,1)S(1)} async-done(((bf16[32,2,3584]{2,1,0:T(2,128)(2,1)}), bf16[32,2,3584]{2,1,0:T(2,128)(2,1)S(1)}, u32[]{:S(2)}, u32[]{:S(2)}) %all-to-all-start) | async-done | bytes 458784 | tf_op jit(solution)/shard_map/all_to_all | solution.py:45
  48.0 4.5 all-to-all-start.4
  57.0 4.9 all-to-all-done.4
  61.9 4.4 all-to-all-start.5
  70.5 5.3 all-to-all-done.5
  75.8 4.1 all-to-all-start.1
  82.2 17.3 %all-to-all-done.1 = bf16[64,7,1024]{2,1,0:T(8,128)(2,1)S(1)} async-done(((bf16[64,7,1024]{2,1,0:T(8,128)(2,1)}), bf16[64,7,1024]{2,1,0:T(8,128)(2,1)S(1)}, u32[]{:S(2)}, u32[]{:S(2)}) %all-to-all-start.1) | async-done | bytes 917536 | tf_op jit(solution)/shard_map/all_to_all | solution.py:66
  99.6 5.1 all-to-all-start.2
  116.1 8.4 %all-to-all-done.2 = bf16[64,7,1024]{2,1,0:T(8,128)(2,1)} async-done(((bf16[64,7,1024]{2,1,0:T(8,128)(2,1)}), bf16[64,7,1024]{2,1,0:T(8,128)(2,1)}, u32[]{:S(2)}, u32[]{:S(2)}) %all-to-all-start.2) | async-done | bytes 917536 | tf_op jit(solution)/shard_map/all_to_all | solution.py:69
  135.0 2.9 fusion.53
  137.9 2.7 fusion.55
  140.5 2.7 convolution_add_fusion.2
  143.3 3.8 fusion.29
  148.9 4.6 all-to-all-start.6
  155.4 10.4 %all-to-all-done.6 = bf16[2,224,1024]{2,0,1:T(2,128)(2,1)S(1)} async-done(((bf16[2,224,1024]{2,0,1:T(2,128)(2,1)}), bf16[2,224,1024]{2,0,1:T(2,128)(2,1)S(1)}, u32[]{:S(2)}, u32[]{:S(2)}) %all-to-all-start.6) | async-done | bytes 917536 | tf_op jit(solution)/shard_map/all_to_all | solution.py:103
  165.8 5.3 all-to-all-start.7
  172.1 17.8 %all-to-all-done.7 = bf16[2,224,1024]{2,0,1:T(2,128)(2,1)S(1)} async-done(((bf16[2,224,1024]{2,0,1:T(2,128)(2,1)}), bf16[2,224,1024]{2,0,1:T(2,128)(2,1)S(1)}, u32[]{:S(2)}, u32[]{:S(2)}) %all-to-all-start.7) | async-done | bytes 917536 | tf_op jit(solution)/shard_map/all_to_all | solution.py:106
  192.4 16.6 %all_to_all.146 = bf16[32,7,1024]{2,1,0:T(8,128)(2,1)S(1)} all-to-all(bf16[32,7,1024]{2,1,0:T(8,128)(2,1)S(1)} %copy.116), channel_id=1, replica_groups=mesh['ctx'=32,'ch'=4] {'ctx'}, dimensions={0} | all-to-all | bytes 917504 | tf_op jit(solution)/shard_map/all_to_all | solution.py:113
  209.0 7.0 stack.2
  216.0 5.1 all-to-all-start.9
  222.2 7.4 %fusion.37 = f32[224,4096]{1,0:T(8,128)} fusion(bf16[1024,4096]{1,0:T(8,128)(2,1)} %param.20, f32[224,1024]{1,0:T(8,128)S(1)} %reshape.179, bf16[224,1024]{1,0:T(8,128)(2,1)S(1)} %copy-done.6), kind=kOutput, calls=%fused_computation.64 | convolution fusion | flops 1879736320 | bytes 13434880 | tf_op jit(solution)/shard_map/dot_general | solution.py:199
  229.5 189.1 %all-to-all-done.9 = bf16[32,224,1024]{2,1,0:T(8,128)(2,1)} async-done(((bf16[32,224,1024]{2,1,0:T(8,128)(2,1)}), bf16[32,224,1024]{2,1,0:T(8,128)(2,1)}, u32[]{:S(2)}, u32[]{:S(2)}) %all-to-all-start.9) | async-done | bytes 14680096 | tf_op jit(solution)/shard_map/all_to_all | solution.py:160
  418.7 14.3 %copy_bitcast_fusion = bf16[32,224,8,128]{3,1,2,0:T(8,128)(2,1)} fusion(bf16[32,224,1024]{2,1,0:T(8,128)(2,1)} %all-to-all-done.9), kind=kLoop, calls=%fused_computation.25 | loop fusion | bytes 29360128 | tf_op jit(solution)/shard_map/while | solution.py:178
  433.0 9.1 %copy.127 = bf16[896,8,8,128]{3,2,1,0:T(8,128)(2,1)S(1)} copy(bf16[896,8,8,128]{3,1,2,0:T(8,128)(2,1)} %bitcast.172) | data formatting | bytes 29360128
  442.1 7.4 %copy.117 = bf16[32,224,8,128]{3,1,2,0:T(8,128)(2,1)} copy(bf16[32,224,8,128]{3,2,1,0:T(8,128)(2,1)S(1)} %bitcast.171) | data formatting | bytes 29360128 | tf_op jit(solution)/shard_map/while | solution.py:178
  449.6 87.9 %while.14 = (s32[]{:T(128)}, f32[8,224]{1,0:T(8,128)S(1)}, f32[8,224]{1,0:T(8,128)S(1)}, f32[8,224,128]{2,1,0:T(8,128)S(1)}, s32[32]{0:T(128)S(1)}, /*index=5*/s...) while((s32[]{:T(128)}, f32[8,224]{1,0:T(8,128)S(1)}, ...), condition=%wide.region_5.6_spmd, body=%wide.region_0.5_spmd.sunk | while | flops 210449120 | bytes 8349351 | solution.py:178
  452.2 4.2 conditional.2
  537.5 7.9 %fusion.19 = bf16[224,4096]{1,0:T(8,128)(2,1)} fusion(f32[224,4096]{1,0:T(8,128)} %fusion.37, bf16[1024,4096]{1,0:T(8,128)(2,1)} %param.21, f32[8,224,128]{2,1,0:T(8,128)S(1)} %get-tuple-element.145, f32[8,224]{1,0:T(8,128)S(1)} %get-tuple-element.146), kind=kOutput, calls=%fused_computation.27 | convolution fusion | flops 1881341952 | bytes 14818304 | tf_op jit(solution)/shard_map/dot_general | solution.py:200
  545.4 174.8 %reduce-scatter.2.cloned.1.call-done = bf16[56,4096]{1,0:T(8,128)(2,1)} async-done(((bf16[224,4096]{1,0:T(8,128)(2,1)}), bf16[56,4096]{1,0:T(8,128)(2,1)}) %reduce-scatter.2.cloned.1.call-update) | async-done | bytes 458768 | tf_op jit(solution)/shard_map/reduce_scatter | solution.py:197
  (220 shorter events, 98.2 us)
Async XLA Ops:
  6.5 214.7 %copy-start = (bf16[224,1024]{1,0:T(8,128)(2,1)S(1)}, bf16[224,1024]{1,0:T(8,128)(2,1)}, u32[]{:S(2)}) copy-start(bf16[224,1024]{1,0:T(8,128)(2,1)} %param.17) | copy-start | bytes 1376260
  6.5 426.4 %all-gather.2.cloned.1.call-start = ((), (), s32[]{:S(2)}) async-start(), calls=%async_computation.11 | async-start | bytes 15138816 | tf_op jit(solution)/shard_map/all_gather | solution.py:157
  10.3 20.1 %all-to-all-start.3 = ((bf16[32,2,224]{2,1,0:T(2,128)(2,1)}), bf16[32,2,224]{2,1,0:T(2,128)(2,1)S(1)}, u32[]{:S(2)}, u32[]{:S(2)}) async-start(bf16[32,2,224]{2,1,0:T(2,128)(2,1)} %reshape.186), calls=%async_computation.3 | async-start | bytes 65536 | tf_op jit(solution)/shard_map/all_to_all | solution.py:48
  30.4 17.5 %all-to-all-start = ((bf16[32,2,3584]{2,1,0:T(2,128)(2,1)}), bf16[32,2,3584]{2,1,0:T(2,128)(2,1)S(1)}, u32[]{:S(2)}, u32[]{:S(2)}) async-start(bf16[32,2,3584]{2,1,0:T(2,128)(2,1)} %reshape.192), calls=%async_computation | async-start | bytes 917504 | tf_op jit(solution)/shard_map/all_to_all | solution.py:45
  48.0 13.9 %all-to-all-start.4 = ((bf16[32,2,448]{2,1,0:T(2,128)(2,1)}), bf16[32,2,448]{2,1,0:T(2,128)(2,1)S(1)}, u32[]{:S(2)}, u32[]{:S(2)}) async-start(bf16[32,2,448]{2,1,0:T(2,128)(2,1)} %reshape.188), calls=%async_computation.4 | async-start | bytes 131072 | tf_op jit(solution)/shard_map/all_to_all | solution.py:72
  61.9 13.9 %all-to-all-start.5 = ((bf16[32,2,448]{2,1,0:T(2,128)(2,1)}), bf16[32,2,448]{2,1,0:T(2,128)(2,1)S(1)}, u32[]{:S(2)}, u32[]{:S(2)}) async-start(bf16[32,2,448]{2,1,0:T(2,128)(2,1)} %reshape.190), calls=%async_computation.5 | async-start | bytes 131072 | tf_op jit(solution)/shard_map/all_to_all | solution.py:75
  70.5 10.2 %copy-start.5 = (bf16[64,7,1024]{2,0,1:T(8,128)(2,1)S(1)}, bf16[64,7,1024]{2,0,1:T(8,128)(2,1)}, u32[]{:S(2)}) copy-start(bf16[64,7,1024]{2,0,1:T(8,128)(2,1)} %get-tuple-element.199) | copy-start | bytes 2752516
  75.8 23.8 %all-to-all-start.1 = ((bf16[64,7,1024]{2,1,0:T(8,128)(2,1)}), bf16[64,7,1024]{2,1,0:T(8,128)(2,1)S(1)}, u32[]{:S(2)}, u32[]{:S(2)}) async-start(bf16[64,7,1024]{2,1,0:T(8,128)(2,1)} %copy.89), calls=%async_computation.1 | async-start | bytes 2097152 | tf_op jit(solution)/shard_map/all_to_all | solution.py:66
  99.6 6.3 copy-start.4
  99.6 24.9 %all-to-all-start.2 = ((bf16[64,7,1024]{2,1,0:T(8,128)(2,1)}), bf16[64,7,1024]{2,1,0:T(8,128)(2,1)}, u32[]{:S(2)}, u32[]{:S(2)}) async-start(bf16[64,7,1024]{2,1,0:T(8,128)(2,1)} %copy.92), calls=%async_computation.2 | async-start | bytes 2097152 | tf_op jit(solution)/shard_map/all_to_all | solution.py:69
  130.5 2.0 copy-start.2
  130.5 2.0 copy-start.3
  148.9 16.9 %all-to-all-start.6 = ((bf16[2,224,1024]{2,0,1:T(2,128)(2,1)}), bf16[2,224,1024]{2,0,1:T(2,128)(2,1)S(1)}, u32[]{:S(2)}, u32[]{:S(2)}) async-start(bf16[2,224,1024]{2,0,1:T(2,128)(2,1)} %copy.112), calls=%async_computation.6 | async-start | bytes 1835008 | tf_op jit(solution)/shard_map/all_to_all | solution.py:103
  165.8 24.1 %all-to-all-start.7 = ((bf16[2,224,1024]{2,0,1:T(2,128)(2,1)}), bf16[2,224,1024]{2,0,1:T(2,128)(2,1)S(1)}, u32[]{:S(2)}, u32[]{:S(2)}) async-start(bf16[2,224,1024]{2,0,1:T(2,128)(2,1)} %copy.114), calls=%async_computation.7 | async-start | bytes 1835008 | tf_op jit(solution)/shard_map/all_to_all | solution.py:106
  191.5 17.5 %copy-start.7 = (bf16[224,1024]{1,0:T(8,128)(2,1)S(1)}, bf16[224,1024]{1,0:T(8,128)(2,1)}, u32[]{:S(2)}) copy-start(bf16[224,1024]{1,0:T(8,128)(2,1)} %param.19) | copy-start | bytes 1376260
  216.0 202.7 %all-to-all-start.9 = ((bf16[32,224,1024]{2,1,0:T(8,128)(2,1)}), bf16[32,224,1024]{2,1,0:T(8,128)(2,1)}, u32[]{:S(2)}, u32[]{:S(2)}) async-start(bf16[32,224,1024]{2,1,0:T(8,128)(2,1)} %stack.2), calls=%async_computation.9 | async-start | bytes 29360128 | tf_op jit(solution)/shard_map/all_to_all | solution.py:160
  221.1 1.0 copy-start.6
  221.2 499.0 %reduce-scatter.2.cloned.1.call-start = ((), (), s32[]{:S(2)}) async-start(), calls=%async_computation.12 | async-start | bytes 2293760 | tf_op jit(solution)/shard_map/reduce_scatter | solution.py:197
  537.5 182.7 %copy-start.1 = (bf16[224,1024]{1,0:T(8,128)(2,1)S(1)}, bf16[224,1024]{1,0:T(8,128)(2,1)}, u32[]{:S(2)}) copy-start(bf16[224,1024]{1,0:T(8,128)(2,1)} %param.17) | copy-start | bytes 1376260
Sparse Core Ops, SparseCore 0:
  10.4 178.2 all-gather.1
  545.5 174.5 reduce-scatter.1
